TPU v7x, 512 devices: a whole 4x4x16 slice. The times are simulated.
512 devices in a mesh: seq: 128 (over y, z, core), head: 4 (over x).
Axes of the slice: x: 4, y: 4, z: 16, core: 2. Of those that a mesh axis runs over, the one named last changes fastest.
Arguments:
- tokens: bfloat16 [64, 4, 1024], P('head'), may hold values from -6 to 6
- cache_keys: bfloat16 [64, 4096, 512], P(None, 'seq', 'head'), may hold values from -70 to 70
- cache_values: bfloat16 [64, 4096, 512], P(None, 'seq', 'head'), may hold values from -6 to 6
- held_states: bfloat16 [64, 512, 1024], P(None, 'seq'), may hold values from -6 to 6
- recompute_pos: int32 [64, 512], P(None, 'seq'), may hold values from 0 to 4095, as said below
- cache_len: int32 [64], replicated, may hold values from 1 to 4096
- new_prompt: int32 [64], replicated, may hold values 0 or 1
- w_qkv: bfloat16 [3, 1024, 512], P(None, None, 'head'), may hold values from -0.1875 to 0.1875
- qkv_bias: float32 [3, 512], P(None, 'head'), may hold values from -3 to 3
- w_out: bfloat16 [512, 1024], P('head'), may hold values from -1.5 to 1.5
- out_bias: float32 [1024], replicated, may hold values from -3 to 3
- attn_gain: float32 [1024], replicated, may hold values from 0.1 to 1.9
- attn_shift: float32 [1024], replicated, may hold values from -3 to 3
- w_up: bfloat16 [1024, 2048], P(None, 'head'), may hold values from -0.1875 to 0.1875
- up_bias: float32 [2048], P('head'), may hold values from -3 to 3
- w_down: bfloat16 [2048, 1024], P('head'), may hold values from -0.125 to 0.125
- down_bias: float32 [1024], replicated, may hold values from -3 to 3
- ffn_gain: float32 [1024], replicated, may hold values from 0.1 to 1.9
- ffn_shift: float32 [1024], replicated, may hold values from -3 to 3
Outputs:
- layer_out: bfloat16 [64, 4, 1024], P('head')
Inputs may be any that keep to these rules, and one draw needn't show every extreme that they name: `recompute_pos`: columns s * 4 to (s + 1) * 4 - 1 of a row hold distinct positions from s * 32 to (s + 1) * 32 - 1.
All inputs are finite; a program needn't handle non-finite values.
Results may differ from a plain program's by a relative error of at most 0.011.
Values may be sent and summed in bfloat16 or wider, within the bound.
No kernel may reach another device: no remote copies, remote signals or barrier semaphores. Data moves between devices by JAX's collectives and lax.ppermute only.
A program may use at most 192 MiB of HBM per device.

v0:
```python
import jax
import jax.numpy as jnp
from jax import lax
from jax.sharding import PartitionSpec as P

HDIM = 64
NEG = -1e30
EPS = 1e-05


def layer_norm(values, norm_gain, norm_bias):
    center = jnp.mean(values, axis=-1, keepdims=True)
    spread = values - center
    second = jnp.mean(spread * spread, axis=-1, keepdims=True)
    return spread * lax.rsqrt(second + EPS) * norm_gain + norm_bias


def merge_pair(first_part, second_part):
    first_max, first_sum, first_out = first_part
    second_max, second_sum, second_out = second_part
    joint_max = jnp.maximum(first_max, second_max)
    first_scale = jnp.exp(first_max - joint_max)
    second_scale = jnp.exp(second_max - joint_max)
    return (
        joint_max,
        first_sum * first_scale + second_sum * second_scale,
        first_out * first_scale[..., None] + second_out * second_scale[..., None],
    )


def partial_attention(queries, keys_here, values_here, visible):
    scores = jnp.einsum(
        "rthe,rphe->rthp", queries, keys_here, preferred_element_type=jnp.float32
    ) * HDIM ** (-0.5)
    highest = jnp.max(jnp.where(visible, scores, NEG), axis=-1)
    weights = jnp.exp(jnp.where(visible, scores - highest[..., None], NEG)).astype(jnp.bfloat16)
    totals = jnp.sum(weights.astype(jnp.float32), axis=-1)
    blended = jnp.einsum(
        "rthp,rphe->rthe", weights, values_here, preferred_element_type=jnp.float32
    )
    return (highest, totals, blended)


def on_device(
    tokens,
    cache_keys,
    cache_values,
    held_states,
    recompute_pos,
    cache_len,
    new_prompt,
    w_qkv,
    qkv_bias,
    w_out,
    out_bias,
    attn_gain,
    attn_shift,
    w_up,
    up_bias,
    w_down,
    down_bias,
    ffn_gain,
    ffn_shift,
):
    local_width = w_qkv.shape[2]
    local_heads = local_width // HDIM
    requests = cache_keys.shape[0]
    block_len = cache_keys.shape[1]
    own_rows = tokens.shape[0]
    steps_count = tokens.shape[1]
    block_rows = lax.all_gather(tokens, "head", axis=0, tiled=True)
    triple = (
        jnp.einsum("rtd,kdc->rtkc", block_rows, w_qkv, preferred_element_type=jnp.float32)
        + qkv_bias
    )
    triple = triple.astype(jnp.bfloat16).reshape(
        block_rows.shape[0], block_rows.shape[1], 3 * local_width
    )
    gathered = jnp.concatenate([triple, block_rows], axis=2)
    head_shape = (requests, steps_count, local_heads, HDIM)
    queries = gathered[:, :, :local_width].reshape(head_shape)
    new_keys = gathered[:, :, local_width : 2 * local_width].reshape(head_shape)
    new_values = gathered[:, :, 2 * local_width : 3 * local_width].reshape(head_shape)
    fresh_keys = (
        jnp.einsum("rjd,dc->rjc", held_states, w_qkv[1], preferred_element_type=jnp.float32)
        + qkv_bias[1]
    ).astype(jnp.bfloat16)
    offset_pos = lax.axis_index("seq") * block_len
    positions = jnp.arange(block_len, dtype=jnp.int32)
    matches = (recompute_pos - offset_pos)[:, :, None] == positions[None, None, :]
    placed = jnp.einsum(
        "rjp,rjc->rpc", matches.astype(jnp.bfloat16), fresh_keys, preferred_element_type=jnp.float32
    ).astype(jnp.bfloat16)
    replaced = jnp.any(matches, axis=1)
    keys_here = jnp.where(replaced[:, :, None], placed, cache_keys).reshape(
        requests, block_len, local_heads, HDIM
    )
    values_here = cache_values.reshape(requests, block_len, local_heads, HDIM)
    visible = ((offset_pos + positions)[None, :] < cache_len[:, None]) & (new_prompt[:, None] == 0)
    block_max, block_sum, block_out = partial_attention(
        queries, keys_here, values_here, visible[:, None, None, :]
    )
    cache_max = lax.pmax(block_max, "seq")
    factor = jnp.exp(block_max - cache_max)
    cache_sum, cache_out = lax.psum((block_sum * factor, block_out * factor[..., None]), "seq")
    order_t = jnp.arange(steps_count, dtype=jnp.int32)
    causal = (order_t[:, None] >= order_t[None, :])[None, :, None, :]
    new_max, new_sum, new_out = partial_attention(queries, new_keys, new_values, causal)
    joint_max, joint_sum, joint_out = merge_pair(
        (cache_max, cache_sum, cache_out), (new_max, new_sum, new_out)
    )
    attended = (
        (joint_out / joint_sum[..., None])
        .astype(jnp.bfloat16)
        .reshape(requests, steps_count, local_width)
    )
    head_terms = jnp.einsum("rtc,cd->rtd", attended, w_out, preferred_element_type=jnp.float32)
    summed = lax.psum(head_terms, "head")
    inputs_all = gathered[:, :, 3 * local_width :]
    normed_all = layer_norm(
        inputs_all.astype(jnp.float32) + summed + out_bias, attn_gain, attn_shift
    ).astype(jnp.bfloat16)
    hidden_all = jax.nn.gelu(
        jnp.einsum("rtd,df->rtf", normed_all, w_up, preferred_element_type=jnp.float32) + up_bias,
        approximate=False,
    ).astype(jnp.bfloat16)
    normed = lax.dynamic_slice_in_dim(normed_all, lax.axis_index("head") * own_rows, own_rows, 0)
    reduced = lax.psum_scatter(
        jnp.einsum("rtf,fd->rtd", hidden_all, w_down, preferred_element_type=jnp.float32),
        "head",
        scatter_dimension=0,
        tiled=True,
    )
    return layer_norm(normed.astype(jnp.float32) + reduced + down_bias, ffn_gain, ffn_shift).astype(
        jnp.bfloat16
    )


def solution(mesh):
    placed = (
        P("head", None, None),
        P(None, "seq", "head"),
        P(None, "seq", "head"),
        P(None, "seq", None),
        P(None, "seq"),
        P(),
        P(),
        P(None, None, "head"),
        P(None, "head"),
        P("head", None),
        P(),
        P(),
        P(),
        P(None, "head"),
        P("head"),
        P("head", None),
        P(),
        P(),
        P(),
    )
    return jax.shard_map(
        on_device, mesh=mesh, in_specs=placed, out_specs=P("head", None, None), check_vma=False
    )
```

profile of v0, /device:TPU:8, one launch (start us, length us, event | category | flops | bytes accessed | tf_op | source)
XLA Modules:
  0.0 722.2 jit_solution(1206370637751851345)
XLA Ops:
  6.5 0.8 copy-done.17
  7.4 0.2 fusion.67
  7.6 0.5 copy-done.16
  8.1 1.5 fusion.9
  9.6 0.9 fusion
  10.5 0.4 reshape.114
  11.0 0.5 copy-done.9
  11.5 13.3 %all_gather.3 = bf16[64,4,1024]{2,0,1:T(8,128)(2,1)S(1)} all-gather(bf16[16,4,1024]{2,0,1:T(8,128)(2,1)S(1)} %copy.59), channel_id=1, replica_groups=mesh['seq'=128,'head'=4] {'head'}, dimensions={0}, use_global_device_ids=true | all-gather | bytes 655360 | tf_op jit(solution)/shard_map/all_gather | solution.py:71
  24.8 0.4 fusion.8
  25.2 0.7 fusion.119
  26.0 0.5 copy-done.22
  26.6 0.6 copy-done.18
  27.3 0.8 select_reduce_fusion
  28.2 0.4 convert_reduce_fusion
  28.7 215.2 %pmax.7 = f32[64,4,2]{0,1,2:T(4,128)S(1)} all-reduce(f32[64,4,2]{0,1,2:T(4,128)S(1)} %copy.68), channel_id=1, replica_groups=mesh['seq'=128,'head'=4] {'seq'}, use_global_device_ids=true, to_apply=%region_2.3 | all-reduce | flops 512 | bytes 4096 | tf_op jit(solution)/shard_map/pmax | solution.py:103
  244.0 0.7 copy.69
  244.7 0.4 reshape.117
  245.1 2.0 fusion.5
  247.2 217.3 %psum.22 = f32[64,4,2]{0,1,2:T(4,128)S(1)} all-reduce(f32[64,4,2]{0,1,2:T(4,128)S(1)} %bitcast.79), channel_id=1, replica_groups=mesh['seq'=128,'head'=4] {'seq'}, use_global_device_ids=true, to_apply=%region_6.7 | all-reduce | flops 512 | bytes 4096 | tf_op jit(solution)/shard_map/psum | solution.py:105
  464.6 0.3 fusion.65
  464.9 0.1 copy.72
  465.1 0.1 fusion.77
  465.2 0.1 convert_reduce_fusion.1
  465.3 0.1 copy.74
  465.4 0.1 copy.78
  465.6 0.1 copy.81
  465.7 0.2 copy.76
  466.0 144.9 %all-reduce.3.cloned.1.call-done = f32[64,4,2,64]{3,1,2,0:T(4,128)} async-done(((f32[64,4,2,64]{3,1,2,0:T(4,128)}), f32[64,4,2,64]{3,1,2,0:T(4,128)}) %all-reduce.3.cloned.1.call-update) | async-done | bytes 131088 | tf_op jit(solution)/shard_map/psum | solution.py:105
  610.9 1.4 fusion.7
  612.4 0.1 copy.82
  612.5 0.1 reshape.120
  612.6 0.7 copy-done.6
  613.3 1.3 fusion.30
  614.7 58.5 %all-reduce.5.cloned.1.call-done = f32[64,4,1024]{2,0,1:T(8,128)} async-done(((f32[64,4,1024]{2,0,1:T(8,128)}), f32[64,4,1024]{2,0,1:T(8,128)}) %all-reduce.5.cloned.1.call-update) | async-done | bytes 1048592 | tf_op jit(solution)/shard_map/psum | solution.py:118
  673.2 1.5 fusion.27
  674.8 0.3 multiply_reduce_fusion
  675.1 0.4 copy-done.13
  675.5 0.3 copy-done.12
  675.8 0.3 add_convert_fusion
  676.1 0.9 copy-done.19
  677.0 0.6 fusion.69
  677.6 2.5 fusion.10
  680.1 32.6 %reduce-scatter.2.cloned.1.call-done = f32[16,4,1024]{2,0,1:T(8,128)} async-done(((f32[64,4,1024]{2,0,1:T(8,128)}), f32[16,4,1024]{2,0,1:T(8,128)}) %reduce-scatter.2.cloned.1.call-update) | async-done | bytes 262160 | tf_op jit(solution)/shard_map/reduce_scatter | solution.py:128
  712.7 1.1 fusion.76
  713.9 0.2 multiply_reduce_fusion.1
  714.1 0.7 copy-done.14
  714.7 0.1 add_convert_fusion.1
  714.9 0.8 copy.83
  (62 shorter events, 1.0 us)
Async XLA Ops:
  6.5 671.0 %copy-start = (bf16[512,1024]{1,0:T(8,128)(2,1)S(1)}, bf16[512,1024]{1,0:T(8,128)(2,1)}, u32[]{:S(2)}) copy-start(bf16[512,1024]{1,0:T(8,128)(2,1)} %param.34) | copy-start | bytes 3145732
  6.5 604.4 %all-reduce.3.cloned.1.call-start = ((), (), s32[]{:S(2)}) async-start(), calls=%async_computation.1 | async-start | bytes 524288 | tf_op jit(solution)/shard_map/psum | solution.py:105
  6.5 0.8 copy-start.17
  7.4 0.7 copy-start.16
  8.1 1.5 copy-start.20
  10.5 0.9 copy-start.9
  11.4 13.3 %copy-start.3 = (bf16[3,1024,128]{2,1,0:T(8,128)(2,1)S(1)}, bf16[3,1024,128]{2,1,0:T(8,128)(2,1)}, u32[]{:S(2)}) copy-start(bf16[3,1024,128]{2,1,0:T(8,128)(2,1)} %param.26) | copy-start | bytes 2359300
  25.9 0.7 copy-start.22
  26.6 0.7 copy-start.7
  26.6 0.7 copy-start.18
  28.1 216.6 %copy-start.4 = (bf16[64,32,128]{2,1,0:T(8,128)(2,1)S(1)}, bf16[64,32,128]{2,1,0:T(8,128)(2,1)}, u32[]{:S(2)}) copy-start(bf16[64,32,128]{2,1,0:T(8,128)(2,1)} %param.21) | copy-start | bytes 1572868
  247.1 217.4 %copy-start.5 = (bf16[64,4,128]{2,0,1:T(8,128)(2,1)S(1)}, bf16[64,4,128]{2,0,1:T(8,128)(2,1)}, u32[]{:S(2)}) copy-start(bf16[64,4,128]{2,0,1:T(8,128)(2,1)} %get-tuple-element.15) | copy-start | bytes 196612
  247.1 217.5 %copy-start.8 = (bf16[64,4,2,64]{3,2,0,1:T(2,128)(2,1)S(1)}, bf16[64,4,2,64]{3,2,0,1:T(2,128)(2,1)}, u32[]{:S(2)}) copy-start(bf16[64,4,2,64]{3,2,0,1:T(2,128)(2,1)} %copy-done.7) | copy-start | bytes 196612
  247.1 426.1 %all-reduce.5.cloned.1.call-start = ((), (), s32[]{:S(2)}) async-start(), calls=%async_computation.2 | async-start | bytes 2097152 | tf_op jit(solution)/shard_map/psum | solution.py:118
  612.4 1.0 copy-start.6
  614.6 58.6 %copy-start.10 = (f32[1024]{0:T(1024)S(1)}, f32[1024]{0:T(1024)}, u32[]{:S(2)}) copy-start(f32[1024]{0:T(1024)} %param.29) | copy-start | bytes 12292
  614.7 98.1 %reduce-scatter.2.cloned.1.call-start = ((), (), s32[]{:S(2)}) async-start(), calls=%async_computation.3 | async-start | bytes 1310720 | tf_op jit(solution)/shard_map/reduce_scatter | solution.py:128
  673.2 1.5 copy-start.1
  674.8 0.7 copy-start.13
  675.1 0.7 copy-start.12
  675.8 1.2 copy-start.19
  675.8 1.2 copy-start.21
  680.1 32.6 %copy-start.11 = (f32[1024]{0:T(1024)S(1)}, f32[1024]{0:T(1024)}, u32[]{:S(2)}) copy-start(f32[1024]{0:T(1024)} %param.35) | copy-start | bytes 12292
  712.7 1.1 copy-start.2
  712.7 1.4 copy-start.15
  714.1 0.7 copy-start.14
Sparse Core Ops, SparseCore 0:
  247.3 363.6 all-reduce.2
  614.8 58.4 all-reduce.4
  680.2 32.4 reduce-scatter.1
where the time goes:
time: 723 us; the launch traced here: 722 us
  blocking collectives  446 us (62%)
  waiting for transfers between devices  236 us (33%)
  between operations  13.4 us (2%)
  matrix products  11.8 us (2%)
  local copies, waits for them, and re-layouts  10.5 us (1%)
    psum x1, blocking collectives, on_device(): lax.psum((block_sum * factor, block_out * factor[..., None]), 'seq')  217 us
    pmax x1, blocking collectives, on_device(): cache_max = lax.pmax(block_max, 'seq')  215 us
    psum x1, waiting for transfers between devices, on_device(): lax.psum((block_sum * factor, block_out * factor[..., None]), 'seq')  145 us
    psum x1, waiting for transfers between devices, on_device(): summed = lax.psum(head_terms, 'head')  58.5 us
    reduce_scatter x1, waiting for transfers between devices, on_device(): lax.psum_scatter(jnp.einsum('rtf,fd->rtd', hidden_all, w_down, preferred_...  32.6 us
  transfers between devices with their start and end apart: 3, of which 3 were waited for; matrix products, arithmetic and copies ran while one was open for 0% of the time, Pallas kernels for 0%

commit v1 on v0

--- a/solution.py
+++ b/solution.py
@@ -1,3 +1,4 @@
+import functools
 import jax
 import jax.numpy as jnp
 from jax import lax
@@ -6,6 +7,24 @@
 HDIM = 64
 NEG = -1e30
 EPS = 1e-05
+
+
+def load_the_masks(obj, along_axis):
+    many = lax.psum(1, along_axis)
+
+    def feed_case_all(right_arr, e_now):
+        if e_now >= many:
+            return right_arr
+        r2 = range(many)
+        even = map(lambda dev_i: (dev_i, dev_i ^ e_now), r2)
+        block_next = list(even)
+        y = lax.ppermute(right_arr, along_axis, block_next)
+        return feed_case_all(right_arr + y, 2 * e_now)
+
+    return feed_case_all(obj, 1)
+
+
+keep_up_target = functools.partial(load_the_masks, along_axis="head")
 
 
 def layer_norm(values, norm_gain, norm_bias):
@@ -115,7 +134,7 @@
         .reshape(requests, steps_count, local_width)
     )
     head_terms = jnp.einsum("rtc,cd->rtd", attended, w_out, preferred_element_type=jnp.float32)
-    summed = lax.psum(head_terms, "head")
+    summed = keep_up_target(head_terms)
     inputs_all = gathered[:, :, 3 * local_width :]
     normed_all = layer_norm(
         inputs_all.astype(jnp.float32) + summed + out_bias, attn_gain, attn_shift

time: 723 us -> 710 us (0.982)
  waiting for transfers between devices: 236 us -> 218 us
  starting transfers between devices: 0.09 us -> 8.31 us
    psum x1 -> x0, waiting for transfers between devices: 58.5 us -> none  [on_device(): summed = lax.psum(head_terms, 'head')]
    ppermute x0 -> x2, waiting for transfers between devices: none -> 43.9 us  [feed_case_all(): y = lax.ppermute(right_arr, along_axis, block_next)]
    ppermute x0 -> x2, starting transfers between devices: none -> 8.27 us  [feed_case_all(): y = lax.ppermute(right_arr, along_axis, block_next)]
  transfers between devices with their start and end apart: 3 -> 4, of which waited for: 3 -> 4; matrix products, arithmetic and copies ran while one was open for 0% -> 0% of each run, Pallas kernels for 0% -> 0%
where the time goes in v1:
time: 710 us
  blocking collectives  446 us (63%)
  waiting for transfers between devices  218 us (31%)
  between operations  13.8 us (2%)
  matrix products  10.8 us (2%)
  local copies, waits for them, and re-layouts  10 us (1%)
  starting transfers between devices  8.31 us (1%)
    psum x1, blocking collectives, on_device(): lax.psum((block_sum * factor, block_out * factor[..., None]), 'seq')  217 us
    pmax x1, blocking collectives, on_device(): cache_max = lax.pmax(block_max, 'seq')  215 us
    psum x1, waiting for transfers between devices, on_device(): lax.psum((block_sum * factor, block_out * factor[..., None]), 'seq')  145 us
    ppermute x2, waiting for transfers between devices, feed_case_all(): y = lax.ppermute(right_arr, along_axis, block_next)  43.9 us
    reduce_scatter x1, waiting for transfers between devices, on_device(): lax.psum_scatter(jnp.einsum('rtf,fd->rtd', hidden_all, w_down, preferred_...  28.9 us
  transfers between devices with their start and end apart: 4, of which 4 were waited for; matrix products, arithmetic and copies ran while one was open for 0% of the time, Pallas kernels for 0%

profile of v1, /device:TPU:8, one launch (start us, length us, event | category | flops | bytes accessed | tf_op | source)
XLA Modules:
  0.0 709.7 jit_solution(1287097058378115641)
XLA Ops:
  6.5 0.8 copy-done.16
  7.4 0.2 fusion.66
  7.6 0.5 copy-done.15
  8.1 1.5 fusion.9
  9.6 0.9 fusion
  10.5 0.4 reshape.114
  11.0 0.5 copy-done.8
  11.5 13.3 %all_gather.3 = bf16[64,4,1024]{2,0,1:T(8,128)(2,1)S(1)} all-gather(bf16[16,4,1024]{2,0,1:T(8,128)(2,1)S(1)} %copy.59), channel_id=1, replica_groups=mesh['seq'=128,'head'=4] {'head'}, dimensions={0}, use_global_device_ids=true | all-gather | bytes 655360 | tf_op jit(solution)/shard_map/all_gather | solution.py:90
  24.8 0.4 fusion.8
  25.2 0.7 fusion.119
  26.0 0.5 copy-done.21
  26.6 0.6 copy-done.17
  27.3 0.8 select_reduce_fusion
  28.2 0.4 convert_reduce_fusion
  28.7 215.2 %pmax.7 = f32[64,4,2]{0,1,2:T(4,128)S(1)} all-reduce(f32[64,4,2]{0,1,2:T(4,128)S(1)} %copy.68), channel_id=1, replica_groups=mesh['seq'=128,'head'=4] {'seq'}, use_global_device_ids=true, to_apply=%region_2.3 | all-reduce | flops 512 | bytes 4096 | tf_op jit(solution)/shard_map/pmax | solution.py:122
  244.0 0.7 copy.69
  244.7 0.4 reshape.117
  245.1 2.0 fusion.5
  247.2 217.3 %psum.15 = f32[64,4,2]{0,1,2:T(4,128)S(1)} all-reduce(f32[64,4,2]{0,1,2:T(4,128)S(1)} %bitcast.79), channel_id=1, replica_groups=mesh['seq'=128,'head'=4] {'seq'}, use_global_device_ids=true, to_apply=%region_6.7 | all-reduce | flops 512 | bytes 4096 | tf_op jit(solution)/shard_map/psum | solution.py:124
  464.6 0.3 fusion.64
  464.9 0.1 copy.72
  465.4 0.1 copy.78
  465.6 0.1 copy.81
  465.7 0.2 copy.76
  466.0 144.9 %all-reduce.2.cloned.1.call-done = f32[64,4,2,64]{3,1,2,0:T(4,128)} async-done(((f32[64,4,2,64]{3,1,2,0:T(4,128)}), f32[64,4,2,64]{3,1,2,0:T(4,128)}) %all-reduce.2.cloned.1.call-update) | async-done | bytes 131088 | tf_op jit(solution)/shard_map/psum | solution.py:124
  610.9 1.4 fusion.7
  612.6 0.7 copy-done.5
  613.3 0.3 fusion.29
  613.6 3.4 collective-permute-start
  617.0 22.4 %collective-permute-done = f32[64,4,1024]{2,0,1:T(8,128)S(1)} collective-permute-done((f32[64,4,1024]{2,0,1:T(8,128)S(1)}, f32[64,4,1024]{2,0,1:T(8,128)S(1)}, u32[]{:S(2)}, u32[]{:S(2)}) %collective-permute-start) | collective-permute-done | bytes 1048608 | tf_op jit(solution)/shard_map/ppermute | solution.py:21
  639.4 0.1 add.126
  639.5 4.9 collective-permute-start.1
  644.4 21.5 %collective-permute-done.1 = f32[64,4,1024]{2,0,1:T(8,128)S(1)} collective-permute-done((f32[64,4,1024]{2,0,1:T(8,128)S(1)}, f32[64,4,1024]{2,0,1:T(8,128)S(1)}, u32[]{:S(2)}, u32[]{:S(2)}) %collective-permute-start.1) | collective-permute-done | bytes 1048608 | tf_op jit(solution)/shard_map/ppermute | solution.py:21
  665.9 0.3 fusion.114
  666.2 0.3 multiply_reduce_fusion
  666.5 0.4 copy-done.11
  666.9 0.3 copy-done.10
  667.1 0.3 add_convert_fusion
  667.4 0.3 copy-done.18
  667.7 0.2 copy-done.20
  667.9 0.6 fusion.68
  668.5 2.5 fusion.10
  671.0 28.9 %reduce-scatter.2.cloned.1.call-done = f32[16,4,1024]{2,0,1:T(8,128)} async-done(((f32[64,4,1024]{2,0,1:T(8,128)}), f32[16,4,1024]{2,0,1:T(8,128)}) %reduce-scatter.2.cloned.1.call-update) | async-done | bytes 262160 | tf_op jit(solution)/shard_map/reduce_scatter | solution.py:147
  700.0 1.1 fusion.75
  701.1 0.2 multiply_reduce_fusion.1
  701.4 0.7 copy-done.12
  702.0 0.1 add_convert_fusion.1
  702.1 0.8 copy.83
  (62 shorter events, 1.5 us)
Async XLA Ops:
  6.5 662.0 %copy-start = (bf16[512,1024]{1,0:T(8,128)(2,1)S(1)}, bf16[512,1024]{1,0:T(8,128)(2,1)}, u32[]{:S(2)}) copy-start(bf16[512,1024]{1,0:T(8,128)(2,1)} %param.34) | copy-start | bytes 3145732
  6.5 604.4 %all-reduce.2.cloned.1.call-start = ((), (), s32[]{:S(2)}) async-start(), calls=%async_computation.1 | async-start | bytes 524288 | tf_op jit(solution)/shard_map/psum | solution.py:124
  6.5 0.8 copy-start.16
  7.4 0.7 copy-start.15
  8.1 1.5 copy-start.19
  10.5 0.9 copy-start.8
  11.4 13.3 %copy-start.2 = (bf16[3,1024,128]{2,1,0:T(8,128)(2,1)S(1)}, bf16[3,1024,128]{2,1,0:T(8,128)(2,1)}, u32[]{:S(2)}) copy-start(bf16[3,1024,128]{2,1,0:T(8,128)(2,1)} %param.26) | copy-start | bytes 2359300
  25.9 0.7 copy-start.21
  26.6 0.7 copy-start.6
  26.6 0.7 copy-start.17
  28.1 216.6 %copy-start.3 = (bf16[64,32,128]{2,1,0:T(8,128)(2,1)S(1)}, bf16[64,32,128]{2,1,0:T(8,128)(2,1)}, u32[]{:S(2)}) copy-start(bf16[64,32,128]{2,1,0:T(8,128)(2,1)} %param.21) | copy-start | bytes 1572868
  247.1 217.4 %copy-start.4 = (bf16[64,4,128]{2,0,1:T(8,128)(2,1)S(1)}, bf16[64,4,128]{2,0,1:T(8,128)(2,1)}, u32[]{:S(2)}) copy-start(bf16[64,4,128]{2,0,1:T(8,128)(2,1)} %get-tuple-element.17) | copy-start | bytes 196612
  247.1 217.5 %copy-start.7 = (bf16[64,4,2,64]{3,2,0,1:T(2,128)(2,1)S(1)}, bf16[64,4,2,64]{3,2,0,1:T(2,128)(2,1)}, u32[]{:S(2)}) copy-start(bf16[64,4,2,64]{3,2,0,1:T(2,128)(2,1)} %copy-done.6) | copy-start | bytes 196612
  247.1 452.8 %reduce-scatter.2.cloned.1.call-start = ((), (), s32[]{:S(2)}) async-start(), calls=%async_computation.2 | async-start | bytes 1310720 | tf_op jit(solution)/shard_map/reduce_scatter | solution.py:147
  612.4 1.0 copy-start.5
  613.6 52.3 %copy-start.14 = (f32[1024]{0:T(1024)S(1)}, f32[1024]{0:T(1024)}, u32[]{:S(2)}) copy-start(f32[1024]{0:T(1024)} %param.29) | copy-start | bytes 12292
  613.6 25.8 %collective-permute-start = (f32[64,4,1024]{2,0,1:T(8,128)S(1)}, f32[64,4,1024]{2,0,1:T(8,128)S(1)}, u32[]{:S(2)}, u32[]{:S(2)}) collective-permute-start(f32[64,4,1024]{2,0,1:T(8,128)S(1)} %fusion.29), channel_id=1, source_target_pairs={{0,1},{1,0},{2,3},{3,2},{4,5},{5,4},{6,7},{7,6},{8,9},{9,8},{10,11... | collective-permute-start | bytes 3145736 | tf_op jit(solution)/shard_map/ppermute | solution.py:21
  639.5 26.4 %collective-permute-start.1 = (f32[64,4,1024]{2,0,1:T(8,128)S(1)}, f32[64,4,1024]{2,0,1:T(8,128)S(1)}, u32[]{:S(2)}, u32[]{:S(2)}) collective-permute-start(f32[64,4,1024]{2,0,1:T(8,128)S(1)} %add.126), channel_id=1, source_target_pairs={{0,2},{1,3},{2,0},{3,1},{4,6},{5,7},{6,4},{7,5},{8,10},{9,11},{10,... | collective-permute-start | bytes 3145736 | tf_op jit(solution)/shard_map/ppermute | solution.py:21
  666.2 0.7 copy-start.11
  666.5 0.7 copy-start.10
  666.5 1.2 copy-start.18
  667.1 0.8 copy-start.20
  671.0 29.0 %copy-start.9 = (f32[1024]{0:T(1024)S(1)}, f32[1024]{0:T(1024)}, u32[]{:S(2)}) copy-start(f32[1024]{0:T(1024)} %param.35) | copy-start | bytes 12292
  700.0 1.1 copy-start.1
  700.0 1.4 copy-start.13
  701.3 0.7 copy-start.12
Sparse Core Ops, SparseCore 0:
  247.3 363.6 all-reduce.1
  671.2 28.7 reduce-scatter.1
